TPU v7x, 256 devices: a whole 4x4x8 slice. The times are simulated.
256 devices in a mesh: blk: 16 (over x_lo, y, core), exp: 16 (over z, x_hi).
Axes of the slice: x: 4 (x_hi: 2, x_lo: 2; x = x_hi * 2 + x_lo), y: 4, z: 8, core: 2. Of those that a mesh axis runs over, the one named last changes fastest.
Arguments:
- hidden: bfloat16 [4096, 2560], P('exp', 'blk'), may hold values from -6 to 6
- attn_gain: float32 [2560], replicated, may hold values from 0.25 to 1.75
- qkv_weight: bfloat16 [2560, 3584], P(None, 'blk'), may hold values from -0.125 to 0.125
- out_weight: bfloat16 [2560, 2560], P(None, 'blk'), may hold values from -0.125 to 0.125
- kv_pool: bfloat16 [16, 64, 128, 1024], P('exp', 'blk'), may hold values from -64 to 64
- page_table: int32 [16, 64], P('exp'), may hold values from 0 to 63, each once within a row
- cache_lens: int32 [16], P('exp'), may hold values from 1 to 7936, as said below
- ffn_gain: float32 [2560], replicated, may hold values from 0.25 to 1.75
- route_ids: int32 [4096, 6], P('exp'), may hold values from 0 to 63, all different within a row; in each aligned block of 256 rows (0 to 255, 256 to 511, ...) at most 32 rows name the same one
- route_weights: float32 [4096, 6], P('exp'), may hold values from 0.05 to 2
- shared_gate_up: bfloat16 [2560, 2, 3072], P(None, None, 'blk'), may hold values from -0.125 to 0.125
- shared_down: bfloat16 [3072, 2560], P('blk'), may hold values from -0.109375 to 0.109375
- expert_gate_up: bfloat16 [256, 2560, 768], P(('blk', 'exp')), may hold values from -0.125 to 0.125
- expert_down: bfloat16 [256, 384, 2560], P(('blk', 'exp')), may hold values from -0.3125 to 0.3125
Outputs:
- hidden_out: bfloat16 [4096, 2560], P('exp', 'blk')
- kv_pool_out: bfloat16 [16, 64, 128, 1024], P('exp', 'blk')
Inputs may be any that keep to these rules, and one draw needn't show every extreme that they name: `route_ids`: among the 256 tokens of one request at most 32 choose any one expert, and some expert is chosen by exactly 32 of them; a token's 6 experts differ. `page_table`: each row names every page of the request's pool once. `cache_lens`: some request has exactly 7936 cached tokens.
All inputs are finite; a program needn't handle non-finite values.
Results may differ from a plain program's by a relative error of at most 0.02.
The roundings to bfloat16 on the way count: a program that leaves them out, or rounds other values in their place, can miss the bound.
Values may be sent and summed in bfloat16 or wider, within the bound.
No kernel may reach another device: no remote copies, remote signals or barrier semaphores. Data moves between devices by JAX's collectives and lax.ppermute only.
A program may use at most 256 MiB of HBM per device.

v0:
```python
import math
import jax
import jax.numpy as jnp
from jax import lax
from jax.sharding import PartitionSpec as P

HEADS = 20
KV_HEADS = 4
HEAD_DIM = 128
TOPK = 6
SPLIT = 4
PAGE = 128
NEW = 256
FF_PART = 384
rope_base = 500000.0
norm_eps = 1e-05


def normalize(inputs, gain_vec):
    values = inputs.astype(jnp.float32)
    inv_rms = lax.rsqrt(jnp.mean(values * values, axis=-1, keepdims=True) + norm_eps)
    return (values * inv_rms * gain_vec).astype(jnp.bfloat16)


def rotate(inputs, positions):
    half_dim = HEAD_DIM // 2
    frequency = rope_base ** (-(jnp.arange(half_dim).astype(jnp.float32) * 2.0 / HEAD_DIM))
    angles = positions.astype(jnp.float32)[:, None] * frequency[None, :]
    cosine = jnp.cos(angles)[:, None, :]
    sine_vals = jnp.sin(angles)[:, None, :]
    lower_half = inputs[..., :half_dim]
    upper_half = inputs[..., half_dim:]
    return jnp.concatenate(
        [
            lower_half * cosine - upper_half * sine_vals,
            upper_half * cosine + lower_half * sine_vals,
        ],
        axis=-1,
    )


def partial_softmax(queries, query_pos, block_rows, key_pos):
    key_width = KV_HEADS * HEAD_DIM
    key_rows = block_rows[:, :key_width].reshape(-1, KV_HEADS, HEAD_DIM)
    value_rows = block_rows[:, key_width:].reshape(-1, KV_HEADS, HEAD_DIM)
    scores = jnp.einsum("tkgd,skd->tkgs", queries, key_rows, preferred_element_type=jnp.float32) * (
        1.0 / math.sqrt(HEAD_DIM)
    )
    allowed = (key_pos[None, :] <= query_pos[:, None])[:, None, None, :]
    maxima = jnp.max(jnp.where(allowed, scores, -1e30), axis=-1)
    weights = jnp.where(allowed, jnp.exp(scores - maxima[..., None]), 0.0)
    totals = jnp.sum(weights, axis=-1)
    weighted = jnp.einsum(
        "tkgs,skd->tkgd",
        weights.astype(jnp.bfloat16),
        value_rows,
        preferred_element_type=jnp.float32,
    )
    return (maxima, totals, weighted)


def per_device(
    hidden,
    attn_gain,
    qkv_weight,
    out_weight,
    kv_pool,
    page_table,
    cache_lens,
    ffn_gain,
    route_ids,
    route_weights,
    shared_gate_up,
    shared_down,
    expert_gate_up,
    expert_down,
):
    blocks = lax.axis_size("blk")
    groups = lax.axis_size("exp")
    block_index = lax.axis_index("blk")
    model_width = hidden.shape[1] * blocks
    query_width = HEADS * HEAD_DIM
    key_width = KV_HEADS * HEAD_DIM
    group_size = HEADS // KV_HEADS
    own_rows = NEW // blocks
    full_rows = lax.all_gather(hidden, "blk", axis=1, tiled=True)
    attn_in = normalize(full_rows, attn_gain)
    projected = jnp.dot(attn_in, qkv_weight, preferred_element_type=jnp.float32).astype(
        jnp.bfloat16
    )
    projected_all = lax.all_gather(projected, "blk", axis=1, tiled=True)
    length = cache_lens[0]
    positions = length + jnp.arange(NEW, dtype=jnp.int32)
    queries = rotate(
        projected_all[:, :query_width].astype(jnp.float32).reshape(NEW, HEADS, HEAD_DIM), positions
    ).astype(jnp.bfloat16)
    fresh_keys = rotate(
        projected_all[:, query_width : query_width + key_width]
        .astype(jnp.float32)
        .reshape(NEW, KV_HEADS, HEAD_DIM),
        positions,
    ).astype(jnp.bfloat16)
    appended = jnp.concatenate(
        [fresh_keys.reshape(NEW, key_width), projected_all[:, query_width + key_width :]], axis=1
    )
    page_map = page_table[0]
    pool_pages = page_map.shape[0]
    page_index = jnp.arange(pool_pages, dtype=jnp.int32)
    logical = jnp.sum(
        jnp.where(page_map[None, :] == page_index[:, None], page_index[None, :], 0), axis=1
    )
    local_pages = kv_pool.shape[1]
    local_logical = lax.dynamic_slice_in_dim(logical, block_index * local_pages, local_pages)
    slot_offsets = jnp.arange(PAGE, dtype=jnp.int32)
    local_pos = local_logical[:, None] * PAGE + slot_offsets[None, :]
    offset = local_pos - length
    written = (offset >= 0) & (offset < NEW)
    picked = appended[jnp.clip(offset, 0, NEW - 1)]
    pool_out = jnp.where(written[:, :, None], picked, kv_pool[0])
    grouped = queries.reshape(NEW, KV_HEADS, group_size, HEAD_DIM)
    slot_rows = pool_out.reshape(local_pages * PAGE, 2 * key_width)
    maxima, totals, weighted = partial_softmax(grouped, positions, slot_rows, local_pos.reshape(-1))
    payload = jnp.concatenate(
        [
            weighted.reshape(NEW, query_width),
            maxima.reshape(NEW, HEADS),
            totals.reshape(NEW, HEADS),
        ],
        axis=1,
    ).reshape(blocks, own_rows, query_width + 2 * HEADS)
    gathered = lax.all_to_all(payload, "blk", split_axis=0, concat_axis=0, tiled=True)
    part_acc = gathered[:, :, :query_width].reshape(blocks, own_rows, HEADS, HEAD_DIM)
    part_max = gathered[:, :, query_width : query_width + HEADS]
    part_sum = gathered[:, :, query_width + HEADS :]
    overall = jnp.max(part_max, axis=0)
    factors = jnp.exp(part_max - overall[None])
    total_sum = jnp.sum(part_sum * factors, axis=0)
    total_acc = jnp.sum(part_acc * factors[..., None], axis=0)
    own_attention = (
        (total_acc / total_sum[..., None]).reshape(own_rows, query_width).astype(jnp.bfloat16)
    )
    attended = jnp.dot(
        lax.all_gather(own_attention, "blk", axis=0, tiled=True),
        out_weight,
        preferred_element_type=jnp.float32,
    )
    mixed_cols = (hidden.astype(jnp.float32) + attended).astype(jnp.bfloat16)
    mixed_rows = lax.all_gather(mixed_cols, "blk", axis=1, tiled=True)
    ffn_in = normalize(mixed_rows, ffn_gain)
    shared_cols = shared_gate_up.shape[2]
    gate_up = jnp.dot(
        ffn_in,
        shared_gate_up.reshape(model_width, 2 * shared_cols),
        preferred_element_type=jnp.float32,
    )
    shared_act = (jax.nn.silu(gate_up[:, :shared_cols]) * gate_up[:, shared_cols:]).astype(
        jnp.bfloat16
    )
    shared_term = jnp.dot(shared_act, shared_down, preferred_element_type=jnp.float32)
    row_experts = groups // SPLIT
    expert_count = row_experts * blocks
    capacity = NEW * TOPK * 4 // (expert_count * 3)
    row_expert_ids = block_index * row_experts + jnp.arange(row_experts, dtype=jnp.int32)
    route_hits = route_ids[:, :, None] == row_expert_ids[None, None, :]
    chosen = jnp.any(route_hits, axis=1)
    route_share = jnp.sum(jnp.where(route_hits, route_weights[:, :, None], 0.0), axis=1)
    slot_rank = jnp.cumsum(chosen.astype(jnp.int32), axis=0) - 1
    slot_ids = jnp.arange(capacity, dtype=jnp.int32)
    placed = chosen.T[:, None, :] & (slot_rank.T[:, None, :] == slot_ids[None, :, None])
    selector = placed.astype(jnp.bfloat16)
    outgoing = jnp.einsum(
        "ect,td->ecd", selector, ffn_in, preferred_element_type=jnp.float32
    ).astype(jnp.bfloat16)
    outgoing = jnp.repeat(outgoing, SPLIT, axis=0)
    received = lax.all_to_all(outgoing, "exp", split_axis=0, concat_axis=0, tiled=True)
    flat_rows = received.reshape(-1, model_width)
    expert_gu = jnp.dot(flat_rows, expert_gate_up[0], preferred_element_type=jnp.float32)
    activated = (jax.nn.silu(expert_gu[:, :FF_PART]) * expert_gu[:, FF_PART:]).astype(jnp.bfloat16)
    result = jnp.dot(activated, expert_down[0], preferred_element_type=jnp.float32).astype(
        jnp.bfloat16
    )
    returned = lax.all_to_all(
        result.reshape(received.shape), "exp", split_axis=0, concat_axis=0, tiled=True
    )
    summed = jnp.sum(
        returned.reshape(row_experts, SPLIT, capacity, model_width).astype(jnp.float32), axis=1
    )
    slot_weight = jnp.sum(placed.astype(jnp.float32) * route_share.T[:, None, :], axis=2)
    slot_values = summed * slot_weight[:, :, None]
    upper_part = slot_values.astype(jnp.bfloat16)
    lower_part = (slot_values - upper_part.astype(jnp.float32)).astype(jnp.bfloat16)
    routed = jnp.einsum(
        "ect,ecd->td", selector, upper_part, preferred_element_type=jnp.float32
    ) + jnp.einsum("ect,ecd->td", selector, lower_part, preferred_element_type=jnp.float32)
    layer_term = shared_term + routed
    summed_cols = lax.psum_scatter(layer_term, "blk", scatter_dimension=1, tiled=True)
    hidden_out = (mixed_cols.astype(jnp.float32) + summed_cols).astype(jnp.bfloat16)
    return (hidden_out, pool_out[None])


def solution(mesh):
    placed = (
        P("exp", "blk"),
        P(),
        P(None, "blk"),
        P(None, "blk"),
        P("exp", "blk", None, None),
        P("exp", None),
        P("exp"),
        P(),
        P("exp", None),
        P("exp", None),
        P(None, None, "blk"),
        P("blk", None),
        P(("blk", "exp"), None, None),
        P(("blk", "exp"), None, None),
    )
    return jax.shard_map(
        per_device,
        mesh=mesh,
        in_specs=placed,
        out_specs=(P("exp", "blk"), P("exp", "blk", None, None)),
        check_vma=False,
    )
```

profile of v0, /device:TPU:4, one launch (start us, length us, event | category | flops | bytes accessed | tf_op | source)
XLA Modules:
  0.0 493.9 jit_solution(17672671257017205096)
XLA Ops:
  8.0 40.1 %all-gather.5.cloned.1.call-done = bf16[256,2560]{0,1:T(8,128)(2,1)} async-done(((bf16[256,160]{0,1:T(8,128)(2,1)}), bf16[256,2560]{0,1:T(8,128)(2,1)}) %all-gather.5.cloned.1.call-update) | async-done | bytes 1310736 | tf_op jit(solution)/shard_map/all_gather | solution.py:86
  49.8 3.0 fusion.34
  55.0 34.1 %all-gather.7.cloned.1.call-done = bf16[256,3584]{0,1:T(8,128)(2,1)} async-done(((bf16[256,224]{0,1:T(8,128)(2,1)}), bf16[256,3584]{0,1:T(8,128)(2,1)}) %all-gather.7.cloned.1.call-update) | async-done | bytes 1835024 | tf_op jit(solution)/shard_map/all_gather | solution.py:91
  99.6 2.3 copy.59
  104.2 8.8 %fusion = (f32[256,4,5]{0,2,1:T(8,128)}, f32[4,512,256,5]{2,1,3,0:T(8,128)}) fusion(pred[256,512]{0,1:T(8,128)(4,1)} %broadcast_compare_fusion, bf16[512,4,128,1]{0,2,3,1:T(8,128)(2,1)S(1)} %bitcast.103, bf16[256,4,5,64]{3,0,2,1:T(8,128)(2,1)} %bitcast.101, bf16[256,4,5,64]{3,0,2,1:T(8,128)(2,1)} %bitcast.100), kind=kOutput, calls=%fused_computation.3 | convolution fusion | flops 681569280 | bytes 12472320 | tf_op jit(solution)/shard_map/tkgd,skd->tkgs/dot_general | solution.py:46
  113.9 6.1 %fusion.3 = f32[256,4,5]{0,2,1:T(8,128)S(1)} fusion(f32[4,512,256,5]{2,1,3,0:T(8,128)} %get-tuple-element.15, f32[256,4,5]{0,2,1:T(8,128)} %get-tuple-element.14, pred[256,512]{0,1:T(8,128)(4,1)} %broadcast_compare_fusion), kind=kLoop, calls=%fused_computation.6 | loop fusion | flops 10480640 | bytes 10657792 | tf_op jit(solution)/shard_map/reduce_sum | solution.py:52
  123.0 7.8 %fusion.22 = f32[256,4,5,128]{0,3,2,1:T(8,128)} fusion(bf16[512,4,128,1]{0,2,3,1:T(8,128)(2,1)} %bitcast.109, f32[4,512,256,5]{2,1,3,0:T(8,128)} %get-tuple-element.15, f32[256,4,5]{0,2,1:T(8,128)S(1)} %copy-done.11, pred[256,512]{0,1:T(8,128)(4,1)S(1)} %copy-done.2), kind=kOutput, calls=%fused_computation.35 | convolution fusion | flops 681574400 | bytes 13783040 | tf_op jit(solution)/shard_map/tkgs,skd->tkgd/dot_general | solution.py:53
  130.9 5.1 %copy.63 = f32[256,4,5,128]{3,2,1,0:T(8,128)} copy(f32[256,4,5,128]{0,3,2,1:T(8,128)} %fusion.22) | data formatting | bytes 5242880 | tf_op jit(solution)/shard_map/tkgs,skd->tkgd/transpose | solution.py:53
  136.0 4.7 concatenate.31
  140.9 4.0 concatenate.34
  145.0 38.8 %all_to_all.15 = f32[16,16,2600]{2,1,0:T(8,128)S(1)} all-to-all(f32[16,16,2600]{2,1,0:T(8,128)} %concatenate.34), channel_id=1, replica_groups=mesh['blk'=16,'exp'=16] {'blk'}, dimensions={0} | all-to-all | bytes 5324800 | tf_op jit(solution)/shard_map/all_to_all | solution.py:131
  187.6 4.2 mul.211
  191.8 2.8 fusion.20
  195.6 34.6 %all-gather.9.cloned.1.call-done = bf16[256,2560]{1,0:T(8,128)(2,1)} async-done(((bf16[16,2560]{1,0:T(8,128)(2,1)}), bf16[256,2560]{1,0:T(8,128)(2,1)}) %all-gather.9.cloned.1.call-update) | async-done | bytes 1310736 | tf_op jit(solution)/shard_map/all_gather | solution.py:143
  230.2 2.7 fusion.37
  234.7 34.0 %all-gather.11.cloned.1.call-done = bf16[256,2560]{0,1:T(8,128)(2,1)} async-done(((bf16[256,160]{0,1:T(8,128)(2,1)}), bf16[256,2560]{0,1:T(8,128)(2,1)}) %all-gather.11.cloned.1.call-update) | async-done | bytes 1310736 | tf_op jit(solution)/shard_map/all_gather | solution.py:148
  272.7 71.8 %all_to_all.16 = bf16[16,32,2560]{2,1,0:T(8,128)(2,1)S(1)} all-to-all(bf16[16,32,2560]{2,1,0:T(8,128)(2,1)S(1)} %bitcast.98), channel_id=1, replica_groups=mesh['blk'=16,'exp'=16] {'exp'}, dimensions={0} | all-to-all | bytes 5242880 | tf_op jit(solution)/shard_map/all_to_all | solution.py:175
  346.7 3.1 convolution_convert_fusion
  349.8 7.2 %all-to-all-start.2 = ((bf16[16,32,2560]{2,1,0:T(8,128)(2,1)}), bf16[16,32,2560]{2,1,0:T(8,128)(2,1)}, u32[]{:S(2)}, u32[]{:S(2)}) async-start(bf16[16,32,2560]{2,1,0:T(8,128)(2,1)} %bitcast.104), calls=%async_computation.2 | async-start | bytes 5242880 | tf_op jit(solution)/shard_map/all_to_all | solution.py:182
  357.2 3.3 fusion.44
  360.5 55.1 %all-to-all-done.2 = bf16[16,32,2560]{2,1,0:T(8,128)(2,1)} async-done(((bf16[16,32,2560]{2,1,0:T(8,128)(2,1)}), bf16[16,32,2560]{2,1,0:T(8,128)(2,1)}, u32[]{:S(2)}, u32[]{:S(2)}) %all-to-all-start.2) | async-done | bytes 2621472 | tf_op jit(solution)/shard_map/all_to_all | solution.py:182
  415.6 2.3 convert_reduce_fusion
  422.2 2.4 broadcast_select_fusion
  424.5 61.3 %reduce-scatter.2.cloned.1.call-done = f32[256,160]{0,1:T(8,128)} async-done(((f32[256,2560]{0,1:T(8,128)}), f32[256,160]{0,1:T(8,128)}) %reduce-scatter.2.cloned.1.call-update) | async-done | bytes 163856 | tf_op jit(solution)/shard_map/reduce_scatter | solution.py:196
  (105 shorter events, 39.3 us)
Async XLA Ops:
  7.2 339.5 %copy-start = (bf16[1,384,2560]{2,1,0:T(8,128)(2,1)S(1)}, bf16[1,384,2560]{2,1,0:T(8,128)(2,1)}, u32[]{:S(2)}) copy-start(bf16[1,384,2560]{2,1,0:T(8,128)(2,1)} %param.27) | copy-start | bytes 5898244
  7.2 40.9 %all-gather.5.cloned.1.call-start = ((), (), s32[]{:S(2)}) async-start(), calls=%async_computation.4 | async-start | bytes 1392640 | tf_op jit(solution)/shard_map/all_gather | solution.py:86
  7.9 45.5 %copy-start.16 = (s32[1,64]{1,0:T(1,128)S(1)}, s32[1,64]{1,0:T(1,128)}, u32[]{:S(2)}) copy-start(s32[1,64]{1,0:T(1,128)} %param.19) | copy-start | bytes 772
  7.9 81.2 %all-gather.7.cloned.1.call-start = ((), (), s32[]{:S(2)}) async-start(), calls=%async_computation.5 | async-start | bytes 1949696 | tf_op jit(solution)/shard_map/all_gather | solution.py:91
  52.7 177.5 %all-gather.9.cloned.1.call-start = ((), (), s32[]{:S(2)}) async-start(), calls=%async_computation.6 | async-start | bytes 1392640 | tf_op jit(solution)/shard_map/all_gather | solution.py:143
  54.2 36.1 %copy-start.5 = (f32[256,64]{0,1:T(8,128)}, f32[256,64]{0,1:T(8,128)S(1)}, u32[]{:S(2)}) copy-start(f32[256,64]{0,1:T(8,128)S(1)} %get-tuple-element.12) | copy-start | bytes 196612
  54.2 36.1 %copy-start.7 = (f32[256,64]{0,1:T(8,128)}, f32[256,64]{0,1:T(8,128)S(1)}, u32[]{:S(2)}) copy-start(f32[256,64]{0,1:T(8,128)S(1)} %get-tuple-element.13) | copy-start | bytes 196612
  96.4 1.4 slice-start
  96.4 1.7 copy-start.6
  96.4 1.7 copy-start.8
  113.9 9.2 %copy-start.2 = (pred[256,512]{0,1:T(8,128)(4,1)S(1)}, pred[256,512]{0,1:T(8,128)(4,1)}, u32[]{:S(2)}) copy-start(pred[256,512]{0,1:T(8,128)(4,1)} %broadcast_compare_fusion) | copy-start | bytes 393220
  113.9 9.1 %copy-start.11 = (f32[256,4,5]{0,2,1:T(8,128)S(1)}, f32[256,4,5]{0,2,1:T(8,128)}, u32[]{:S(2)}) copy-start(f32[256,4,5]{0,2,1:T(8,128)} %get-tuple-element.14) | copy-start | bytes 61444
  136.0 4.9 copy-start.9
  183.8 1.6 copy-start.1
  191.8 38.4 %copy-start.10 = (bf16[256,160]{0,1:T(8,128)(2,1)S(1)}, bf16[256,160]{0,1:T(8,128)(2,1)}, u32[]{:S(2)}) copy-start(bf16[256,160]{0,1:T(8,128)(2,1)} %param.14) | copy-start | bytes 245764
  194.7 38.3 %copy-start.12 = (s32[256,6]{0,1:T(8,128)S(1)}, s32[256,6]{0,1:T(8,128)}, u32[]{:S(2)}) copy-start(s32[256,6]{0,1:T(8,128)} %param.22) | copy-start | bytes 18436
  194.7 75.8 %copy-start.15 = (f32[2560]{0:T(1024)S(1)}, f32[2560]{0:T(1024)}, u32[]{:S(2)}) copy-start(f32[2560]{0:T(1024)} %param.21) | copy-start | bytes 30724
  195.5 73.2 %all-gather.11.cloned.1.call-start = ((), (), s32[]{:S(2)}) async-start(), calls=%async_computation.7 | async-start | bytes 1392640 | tf_op jit(solution)/shard_map/all_gather | solution.py:148
  272.7 71.8 %copy-start.14 = (bf16[1,2560,768]{2,1,0:T(8,128)(2,1)S(1)}, bf16[1,2560,768]{2,1,0:T(8,128)(2,1)}, u32[]{:S(2)}) copy-start(bf16[1,2560,768]{2,1,0:T(8,128)(2,1)} %param.26) | copy-start | bytes 11796484
  349.8 7.2 %copy-start.13 = (f32[256,6]{0,1:T(8,128)S(1)}, f32[256,6]{0,1:T(8,128)}, u32[]{:S(2)}) copy-start(f32[256,6]{0,1:T(8,128)} %param.23) | copy-start | bytes 18436
  349.8 65.8 %all-to-all-start.2 = ((bf16[16,32,2560]{2,1,0:T(8,128)(2,1)}), bf16[16,32,2560]{2,1,0:T(8,128)(2,1)}, u32[]{:S(2)}, u32[]{:S(2)}) async-start(bf16[16,32,2560]{2,1,0:T(8,128)(2,1)} %bitcast.104), calls=%async_computation.2 | async-start | bytes 5242880 | tf_op jit(solution)/shard_map/all_to_all | solution.py:182
  356.9 128.9 %reduce-scatter.2.cloned.1.call-start = ((), (), s32[]{:S(2)}) async-start(), calls=%async_computation.8 | async-start | bytes 2785280 | tf_op jit(solution)/shard_map/reduce_scatter | solution.py:196
  418.6 1.2 copy-start.3
  422.0 63.8 %copy-start.4 = (bf16[256,160]{0,1:T(8,128)(2,1)S(1)}, bf16[256,160]{0,1:T(8,128)(2,1)}, u32[]{:S(2)}) copy-start(bf16[256,160]{0,1:T(8,128)(2,1)} %fusion.37) | copy-start | bytes 245764
Sparse Core Ops, SparseCore 0:
  9.9 38.1 all-gather.4
  52.9 36.1 all-gather.6
  195.6 34.5 all-gather.8
  233.1 35.6 all-gather.10
  422.2 63.5 reduce-scatter.1
where the time goes:
time: 495 us; the launch traced here: 494 us
  waiting for transfers between devices  260 us (53%)
  blocking collectives  111 us (22%)
  local copies, waits for them, and re-layouts  38.8 us (8%)
  matrix products  36.3 us (7%)
  other arithmetic  26 us (5%)
  between operations  14.8 us (3%)
  starting transfers between devices  7.37 us (1%)
    all_to_all x1, blocking collectives, per_device(): lax.all_to_all(outgoing, 'exp', split_axis=0, concat_axis=0, tiled=True)  71.8 us
    reduce_scatter x1, waiting for transfers between devices, per_device(): lax.psum_scatter(layer_term, 'blk', scatter_dimension=1, tiled=True)  61.3 us
    all_to_all x1, waiting for transfers between devices, per_device(): lax.all_to_all(result.reshape(received.shape), 'exp', split_axis=0, conca...  55.1 us
    all_gather x1, waiting for transfers between devices, per_device(): full_rows = lax.all_gather(hidden, 'blk', axis=1, tiled=True)  40.1 us
    all_to_all x1, blocking collectives, per_device(): lax.all_to_all(payload, 'blk', split_axis=0, concat_axis=0, tiled=True)  38.8 us
    all_gather x1, waiting for transfers between devices, per_device(): lax.all_gather(own_attention, 'blk', axis=0, tiled=True)  34.6 us
    all_gather x1, waiting for transfers between devices, per_device(): projected_all = lax.all_gather(projected, 'blk', axis=1, tiled=True)  34.1 us
    all_gather x1, waiting for transfers between devices, per_device(): mixed_rows = lax.all_gather(mixed_cols, 'blk', axis=1, tiled=True)  34 us
  transfers between devices with their start and end apart: 6, of which 6 were waited for; matrix products, arithmetic and copies ran while one was open for 2% of the time, Pallas kernels for 0%

commit v1 on v0

--- a/solution.py
+++ b/solution.py
@@ -145,7 +145,9 @@
         preferred_element_type=jnp.float32,
     )
     mixed_cols = (hidden.astype(jnp.float32) + attended).astype(jnp.bfloat16)
-    mixed_rows = lax.all_gather(mixed_cols, "blk", axis=1, tiled=True)
+    mixed_rows = jnp.concatenate(
+        lax.all_to_all(jnp.stack([mixed_cols] * lax.axis_size("blk")), "blk", 0, 0), axis=1
+    )
     ffn_in = normalize(mixed_rows, ffn_gain)
     shared_cols = shared_gate_up.shape[2]
     gate_up = jnp.dot(

time: 495 us -> 477 us (0.964)
  waiting for transfers between devices: 260 us -> 245 us
  matrix products: 36.3 us -> 30.8 us
    all_gather x1 -> x0, waiting for transfers between devices: 34 us -> none  [per_device(): mixed_rows = lax.all_gather(mixed_cols, 'blk', axis=1, tiled=True)]
    all_to_all x0 -> x1, waiting for transfers between devices: none -> 17.7 us  [per_device(): lax.all_to_all(jnp.stack([mixed_cols] * lax.axis_size('blk')), 'blk', 0, 0)]
where the time goes in v1:
time: 477 us; the launch traced here: 476 us
  waiting for transfers between devices  245 us (51%)
  blocking collectives  109 us (23%)
  local copies, waits for them, and re-layouts  39.2 us (8%)
  matrix products  30.8 us (6%)
  other arithmetic  25.9 us (5%)
  between operations  14.8 us (3%)
  starting transfers between devices  11.7 us (2%)
    all_to_all x1, blocking collectives, per_device(): lax.all_to_all(outgoing, 'exp', split_axis=0, concat_axis=0, tiled=True)  70.3 us
    reduce_scatter x1, waiting for transfers between devices, per_device(): lax.psum_scatter(layer_term, 'blk', scatter_dimension=1, tiled=True)  60.9 us
    all_to_all x1, waiting for transfers between devices, per_device(): lax.all_to_all(result.reshape(received.shape), 'exp', split_axis=0, conca...  56.4 us
    all_gather x1, waiting for transfers between devices, per_device(): full_rows = lax.all_gather(hidden, 'blk', axis=1, tiled=True)  40.1 us
    all_to_all x1, blocking collectives, per_device(): lax.all_to_all(payload, 'blk', split_axis=0, concat_axis=0, tiled=True)  38.8 us
    all_gather x1, waiting for transfers between devices, per_device(): lax.all_gather(own_attention, 'blk', axis=0, tiled=True)  34.7 us
    all_gather x1, waiting for transfers between devices, per_device(): projected_all = lax.all_gather(projected, 'blk', axis=1, tiled=True)  34.1 us
    all_to_all x1, waiting for transfers between devices, per_device(): lax.all_to_all(jnp.stack([mixed_cols] * lax.axis_size('blk')), 'blk', 0, 0)  17.7 us
  transfers between devices with their start and end apart: 6, of which 6 were waited for; matrix products, arithmetic and copies ran while one was open for 2% of the time, Pallas kernels for 0%

profile of v1, /device:TPU:4, one launch (start us, length us, event | category | flops | bytes accessed | tf_op | source)
XLA Modules:
  0.0 476.1 jit_solution(7691558595053567446)
XLA Ops:
  8.0 40.1 %all-gather.4.cloned.1.call-done = bf16[256,2560]{0,1:T(8,128)(2,1)} async-done(((bf16[256,160]{0,1:T(8,128)(2,1)}), bf16[256,2560]{0,1:T(8,128)(2,1)}) %all-gather.4.cloned.1.call-update) | async-done | bytes 1310736 | tf_op jit(solution)/shard_map/all_gather | solution.py:86
  49.8 3.0 fusion.33
  55.0 34.1 %all-gather.6.cloned.1.call-done = bf16[256,3584]{0,1:T(8,128)(2,1)} async-done(((bf16[256,224]{0,1:T(8,128)(2,1)}), bf16[256,3584]{0,1:T(8,128)(2,1)}) %all-gather.6.cloned.1.call-update) | async-done | bytes 1835024 | tf_op jit(solution)/shard_map/all_gather | solution.py:91
  101.8 2.3 copy.60
  104.1 7.9 %fusion = (f32[256,4,5]{0,2,1:T(8,128)S(1)}, f32[4,512,256,5]{2,1,3,0:T(8,128)}) fusion(pred[256,512]{0,1:T(8,128)(4,1)S(1)} %copy-done.4, bf16[512,4,128,1]{0,2,3,1:T(8,128)(2,1)} %bitcast.116, bf16[256,4,5,64]{3,0,2,1:T(8,128)(2,1)} %bitcast.113, bf16[256,4,5,64]{3,0,2,1:T(8,128)(2,1)S(1)} %bitcast.112), kind=kOutput, calls=%fused_computation.3 | convolution fusion | flops 681569280 | bytes 12472320 | tf_op jit(solution)/shard_map/tkgd,skd->tkgs/dot_general | solution.py:46
  112.2 6.1 %fusion.3 = f32[256,4,5]{0,2,1:T(8,128)S(1)} fusion(f32[4,512,256,5]{2,1,3,0:T(8,128)} %get-tuple-element.15, f32[256,4,5]{0,2,1:T(8,128)S(1)} %get-tuple-element.14, pred[256,512]{0,1:T(8,128)(4,1)S(1)} %copy-done.4), kind=kLoop, calls=%fused_computation.6 | loop fusion | flops 10480640 | bytes 10657792 | tf_op jit(solution)/shard_map/reduce_sum | solution.py:52
  119.6 7.8 %fusion.21 = f32[256,4,5,128]{0,3,2,1:T(8,128)} fusion(bf16[512,4,128,1]{0,2,3,1:T(8,128)(2,1)} %bitcast.123, f32[4,512,256,5]{2,1,3,0:T(8,128)} %get-tuple-element.15, f32[256,4,5]{0,2,1:T(8,128)S(1)} %get-tuple-element.14, pred[256,512]{0,1:T(8,128)(4,1)S(1)} %copy-done.4), kind=kOutput, calls=%fused_computation.35 | convolution fusion | flops 681574400 | bytes 13783040 | tf_op jit(solution)/shard_map/tkgs,skd->tkgd/dot_general | solution.py:53
  127.5 5.1 %copy.63 = f32[256,4,5,128]{3,2,1,0:T(8,128)} copy(f32[256,4,5,128]{0,3,2,1:T(8,128)} %fusion.21) | data formatting | bytes 5242880 | tf_op jit(solution)/shard_map/tkgs,skd->tkgd/transpose | solution.py:53
  132.6 4.7 concatenate.31
  137.5 4.0 concatenate.34
  141.5 38.8 %all_to_all.20 = f32[16,16,2600]{2,1,0:T(8,128)S(1)} all-to-all(f32[16,16,2600]{2,1,0:T(8,128)} %concatenate.34), channel_id=1, replica_groups=mesh['blk'=16,'exp'=16] {'blk'}, dimensions={0} | all-to-all | bytes 5324800 | tf_op jit(solution)/shard_map/all_to_all | solution.py:131
  184.2 4.2 mul.229
  188.4 2.9 fusion.17
  192.1 34.7 %all-gather.8.cloned.1.call-done = bf16[256,2560]{1,0:T(8,128)(2,1)} async-done(((bf16[16,2560]{1,0:T(8,128)(2,1)}), bf16[256,2560]{1,0:T(8,128)(2,1)}) %all-gather.8.cloned.1.call-update) | async-done | bytes 1310736 | tf_op jit(solution)/shard_map/all_gather | solution.py:143
  229.9 3.9 all-to-all-start.1
  235.6 17.7 %all-to-all-done.1 = bf16[16,256,160]{1,2,0:T(8,128)(2,1)S(1)} async-done(((bf16[16,256,160]{1,2,0:T(8,128)(2,1)}), bf16[16,256,160]{1,2,0:T(8,128)(2,1)S(1)}, u32[]{:S(2)}, u32[]{:S(2)}) %all-to-all-start.1) | async-done | bytes 1310752 | tf_op jit(solution)/shard_map/all_to_all | solution.py:149
  255.0 70.3 %all_to_all.21 = bf16[16,32,2560]{2,1,0:T(8,128)(2,1)S(1)} all-to-all(bf16[16,32,2560]{2,1,0:T(8,128)(2,1)S(1)} %bitcast.110), channel_id=1, replica_groups=mesh['blk'=16,'exp'=16] {'exp'}, dimensions={0} | all-to-all | bytes 5242880 | tf_op jit(solution)/shard_map/all_to_all | solution.py:177
  327.4 3.1 convolution_convert_fusion
  330.5 7.6 %all-to-all-start.3 = ((bf16[16,32,2560]{2,1,0:T(8,128)(2,1)}), bf16[16,32,2560]{2,1,0:T(8,128)(2,1)}, u32[]{:S(2)}, u32[]{:S(2)}) async-start(bf16[16,32,2560]{2,1,0:T(8,128)(2,1)} %bitcast.117), calls=%async_computation.3 | async-start | bytes 5242880 | tf_op jit(solution)/shard_map/all_to_all | solution.py:184
  340.7 56.4 %all-to-all-done.3 = bf16[16,32,2560]{2,1,0:T(8,128)(2,1)} async-done(((bf16[16,32,2560]{2,1,0:T(8,128)(2,1)}), bf16[16,32,2560]{2,1,0:T(8,128)(2,1)}, u32[]{:S(2)}, u32[]{:S(2)}) %all-to-all-start.3) | async-done | bytes 2621472 | tf_op jit(solution)/shard_map/all_to_all | solution.py:184
  397.1 2.3 convert_reduce_fusion
  401.3 2.3 convolution_add_fusion
  404.8 2.4 broadcast_select_fusion
  407.2 60.9 %reduce-scatter.2.cloned.1.call-done = f32[256,160]{0,1:T(8,128)} async-done(((f32[256,2560]{0,1:T(8,128)}), f32[256,160]{0,1:T(8,128)}) %reduce-scatter.2.cloned.1.call-update) | async-done | bytes 163856 | tf_op jit(solution)/shard_map/reduce_scatter | solution.py:198
  (111 shorter events, 38.6 us)
Async XLA Ops:
  7.2 320.3 %copy-start = (bf16[1,384,2560]{2,1,0:T(8,128)(2,1)S(1)}, bf16[1,384,2560]{2,1,0:T(8,128)(2,1)}, u32[]{:S(2)}) copy-start(bf16[1,384,2560]{2,1,0:T(8,128)(2,1)} %param.27) | copy-start | bytes 5898244
  7.2 40.9 %all-gather.4.cloned.1.call-start = ((), (), s32[]{:S(2)}) async-start(), calls=%async_computation.5 | async-start | bytes 1392640 | tf_op jit(solution)/shard_map/all_gather | solution.py:86
  7.9 45.5 %copy-start.18 = (s32[1,64]{1,0:T(1,128)S(1)}, s32[1,64]{1,0:T(1,128)}, u32[]{:S(2)}) copy-start(s32[1,64]{1,0:T(1,128)} %param.19) | copy-start | bytes 772
  7.9 81.2 %all-gather.6.cloned.1.call-start = ((), (), s32[]{:S(2)}) async-start(), calls=%async_computation.6 | async-start | bytes 1949696 | tf_op jit(solution)/shard_map/all_gather | solution.py:91
  52.7 174.1 %all-gather.8.cloned.1.call-start = ((), (), s32[]{:S(2)}) async-start(), calls=%async_computation.7 | async-start | bytes 1392640 | tf_op jit(solution)/shard_map/all_gather | solution.py:143
  54.2 36.1 %copy-start.9 = (f32[256,64]{0,1:T(8,128)}, f32[256,64]{0,1:T(8,128)S(1)}, u32[]{:S(2)}) copy-start(f32[256,64]{0,1:T(8,128)S(1)} %get-tuple-element.12) | copy-start | bytes 196612
  54.2 36.1 %copy-start.11 = (f32[256,64]{0,1:T(8,128)}, f32[256,64]{0,1:T(8,128)S(1)}, u32[]{:S(2)}) copy-start(f32[256,64]{0,1:T(8,128)S(1)} %get-tuple-element.13) | copy-start | bytes 196612
  92.6 2.7 copy-start.2
  97.7 0.9 copy-start.12
  100.1 4.0 copy-start.4
  112.1 6.4 %copy-start.5 = (bf16[512,512]{1,0:T(8,128)(2,1)S(1)}, bf16[512,512]{1,0:T(8,128)(2,1)}, u32[]{:S(2)}) copy-start(bf16[512,512]{1,0:T(8,128)(2,1)} %get-tuple-element.9) | copy-start | bytes 1572868
  180.4 1.6 copy-start.1
  188.4 38.4 %copy-start.8 = (bf16[2560,160]{0,1:T(8,128)(2,1)S(1)}, bf16[2560,160]{0,1:T(8,128)(2,1)}, u32[]{:S(2)}) copy-start(bf16[2560,160]{0,1:T(8,128)(2,1)} %param.17) | copy-start | bytes 2457604
  188.4 38.4 %copy-start.13 = (bf16[256,160]{0,1:T(8,128)(2,1)S(1)}, bf16[256,160]{0,1:T(8,128)(2,1)}, u32[]{:S(2)}) copy-start(bf16[256,160]{0,1:T(8,128)(2,1)} %param.14) | copy-start | bytes 245764
  192.1 41.8 %copy-start.15 = (s32[256,6]{0,1:T(8,128)S(1)}, s32[256,6]{0,1:T(8,128)}, u32[]{:S(2)}) copy-start(s32[256,6]{0,1:T(8,128)} %param.22) | copy-start | bytes 18436
  228.7 25.0 %copy-start.14 = (f32[2560]{0:T(1024)S(1)}, f32[2560]{0:T(1024)}, u32[]{:S(2)}) copy-start(f32[2560]{0:T(1024)} %param.21) | copy-start | bytes 30724
  229.9 23.4 %all-to-all-start.1 = ((bf16[16,256,160]{1,2,0:T(8,128)(2,1)}), bf16[16,256,160]{1,2,0:T(8,128)(2,1)S(1)}, u32[]{:S(2)}, u32[]{:S(2)}) async-start(bf16[16,256,160]{1,2,0:T(8,128)(2,1)} %stack.2), calls=%async_computation.1 | async-start | bytes 2621440 | tf_op jit(solution)/shard_map/all_to_all | solution.py:149
  254.9 70.3 %copy-start.17 = (bf16[1,2560,768]{2,1,0:T(8,128)(2,1)S(1)}, bf16[1,2560,768]{2,1,0:T(8,128)(2,1)}, u32[]{:S(2)}) copy-start(bf16[1,2560,768]{2,1,0:T(8,128)(2,1)} %param.26) | copy-start | bytes 11796484
  330.5 7.7 %copy-start.16 = (f32[256,6]{0,1:T(8,128)S(1)}, f32[256,6]{0,1:T(8,128)}, u32[]{:S(2)}) copy-start(f32[256,6]{0,1:T(8,128)} %param.23) | copy-start | bytes 18436
  330.5 66.6 %all-to-all-start.3 = ((bf16[16,32,2560]{2,1,0:T(8,128)(2,1)}), bf16[16,32,2560]{2,1,0:T(8,128)(2,1)}, u32[]{:S(2)}, u32[]{:S(2)}) async-start(bf16[16,32,2560]{2,1,0:T(8,128)(2,1)} %bitcast.117), calls=%async_computation.3 | async-start | bytes 5242880 | tf_op jit(solution)/shard_map/all_to_all | solution.py:184
  338.1 129.9 %reduce-scatter.2.cloned.1.call-start = ((), (), s32[]{:S(2)}) async-start(), calls=%async_computation.8 | async-start | bytes 2785280 | tf_op jit(solution)/shard_map/reduce_scatter | solution.py:198
  338.3 1.5 copy-start.6
  400.1 1.2 copy-start.7
  403.6 1.2 copy-start.3
  (1 other events, 0.8 us)
Sparse Core Ops, SparseCore 0:
  9.9 38.1 all-gather.3
  52.9 36.1 all-gather.5
  192.2 34.5 all-gather.7
  403.7 64.2 reduce-scatter.1
